TPU v7x, 128 devices: a whole 4x4x4 slice. The times are simulated.
128 devices in a mesh: row: 8 (over z, core), col: 16 (over y, x).
Axes of the slice: x: 4, y: 4, z: 4, core: 2. Of those that a mesh axis runs over, the one named last changes fastest.
Arguments:
- psi_val: float32 [64, 128, 128, 128], P(None, 'row', 'col'), may hold values from -6 to 6
- psi_cond: float32 [64, 128, 128, 128], P(None, 'row', 'col'), may hold values from -6 to 6
- eps_val: float32 [64], replicated, may hold values from -12 to -1
- eps_cond: float32 [64], replicated, may hold values from 1 to 12
- val_index: int32 [128], replicated, may hold values from 0 to 63
- cond_index: int32 [128], replicated, may hold values from 0 to 63
- gmap: int32 [8192], replicated, may hold values from 0 to 2097151, as said below
- chi0_in: float32 [2, 8192, 8192], P(None, 'row', 'col'), may hold values from -6 to 6
Outputs:
- chi0_out: float32 [2, 8192, 8192], P(None, 'row', 'col')
Inputs may be any that keep to these rules, and one draw needn't show every extreme that they name: gmap holds 8192 distinct entries. Entries g of device block d = g // 64 (d = r * 16 + c) have ky in [r * 16, (r + 1) * 16) and kz in [c * 8, (c + 1) * 8); kx is any.
All inputs are finite; a program needn't handle non-finite values.
Results may differ from a plain program's by a relative error of at most 0.000068.
Values sent between devices are 32-bit elements; how exact they have to be, the bound alone decides.
No kernel may reach another device: no remote copies, remote signals or barrier semaphores. Data moves between devices by JAX's collectives and lax.ppermute only.
A program may use at most 128 MiB of HBM per device.

v0:
```python
import math

import jax
import numpy as np
import jax.numpy as jnp
from jax import lax
from jax.sharding import PartitionSpec as P

GRID = 128
NG = 8192


HIGH = lax.Precision.HIGHEST


def phase_table(left, right, length):
    phase = left[:, None] * right[None, :] % length
    angle = phase.astype(jnp.float32) * (2.0 * math.pi / length)
    return (jnp.cos(angle), jnp.sin(angle))


def contract_pairs(left, right):
    return lax.dot_general(
        left, right, (((0,), (0,)), ((), ())), precision=HIGH, preferred_element_type=jnp.float32
    )


def on_device(psi_val, psi_cond, eps_val, eps_cond, val_index, cond_index, gmap, chi0_in):
    pairs = val_index.shape[0]
    scale = 1.0 / math.sqrt(GRID**3)
    row_pos = lax.axis_index("row")
    col_pos = lax.axis_index("col")
    mesh_cols = lax.axis_size("col")
    mesh_rows = lax.axis_size("row")
    per_device = NG // (mesh_rows * mesh_cols)
    row_span = GRID // mesh_rows
    col_span = GRID // mesh_cols
    steps = jnp.arange(GRID, dtype=jnp.int32)

    halves = 2
    half_pairs = pairs // halves
    mirror = mesh_cols - 1 - col_pos
    low = jnp.minimum(col_pos, mirror)
    side = col_pos // (mesh_cols // 2)
    span_z = col_span + 1
    by_block = gmap.reshape(mesh_rows, mesh_cols, per_device)
    direct = lax.dynamic_index_in_dim(by_block, low, axis=1, keepdims=False)
    mirrored = lax.dynamic_index_in_dim(by_block, mesh_cols - 1 - low, axis=1, keepdims=False)
    both = jnp.stack([direct, mirrored], axis=1).reshape(-1)
    flip = (jnp.arange(both.shape[0], dtype=jnp.int32) // per_device) % 2
    freq_x = both // (GRID * GRID)
    freq_y = both // GRID % GRID
    freq_z = both % GRID
    freq_x = jnp.where(flip == 1, (GRID - freq_x) % GRID, freq_x)
    freq_y = jnp.where(flip == 1, (GRID - freq_y) % GRID, freq_y)
    freq_z = jnp.where(flip == 1, (GRID - freq_z) % GRID, freq_z) - low * col_span
    sign = jnp.where(flip == 1, -1.0, 1.0).astype(jnp.float32)
    pick = freq_y * span_z + freq_z
    x_glob = row_pos * row_span + jnp.arange(row_span, dtype=jnp.int32)
    cos_x, sin_x = phase_table(x_glob, freq_x, GRID)

    kz_set = (jnp.arange(mesh_cols // 2, dtype=jnp.int32)[:, None] * col_span
              + jnp.arange(span_z, dtype=jnp.int32)[None, :]).reshape(-1)
    cos_z, sin_z = phase_table(steps, kz_set, GRID)
    table_z = jnp.stack([cos_z, -sin_z], axis=-1).reshape(GRID, mesh_cols // 2, span_z, 2)
    table_z = jnp.stack([table_z, table_z[:, ::-1]], axis=0)
    cos_y, sin_y = phase_table(steps, steps, GRID)
    table_y = jnp.stack(
        [jnp.stack([cos_y, -sin_y], axis=-1), jnp.stack([sin_y, cos_y], axis=-1)], axis=1
    ).reshape(mesh_cols, col_span, 2, GRID, 2)

    chunks = 4
    chunk = row_span // chunks
    partial = None
    for i in range(chunks):
        xs = slice(i * chunk, (i + 1) * chunk)
        rho = jnp.take(psi_val[:, xs], val_index, axis=0) * jnp.take(psi_cond[:, xs], cond_index, axis=0)
        rho = rho.reshape((halves, half_pairs) + rho.shape[1:])
        z_all = jnp.einsum("hpxyz,hzcjt->hcpxyjt", rho, table_z, precision=HIGH)
        z_all = z_all.reshape((mesh_cols,) + z_all.shape[2:])
        z_mine = lax.all_to_all(z_all, "col", split_axis=0, concat_axis=0, tiled=True)
        y_all = jnp.einsum("spxyjt,syteu->pxeju", z_mine, table_y, precision=HIGH)
        flat = y_all.reshape(half_pairs, chunk, GRID * span_z, 2)
        chosen = jnp.take(flat, pick, axis=2)
        c_re = chosen[..., 0]
        c_im = chosen[..., 1]
        cx = cos_x[xs]
        sx = sin_x[xs]
        part_re = jnp.sum(c_re * cx[None] + c_im * sx[None], axis=1)
        part_im = jnp.sum(c_im * cx[None] - c_re * sx[None], axis=1)
        piece = jnp.stack([part_re, part_im], axis=0)
        partial = piece if partial is None else partial + piece
    partial = partial * jnp.stack([jnp.ones_like(sign), sign])[:, None, :] * scale
    block = 2 * per_device
    spread = partial.reshape(2, half_pairs, mesh_rows, block).transpose(2, 0, 1, 3)
    gathered = lax.all_to_all(spread, "row", split_axis=0, concat_axis=0, tiled=True)
    own = jnp.sum(gathered, axis=0).reshape(2, half_pairs, 2, per_device)
    copies = jnp.broadcast_to(own[None], (mesh_cols,) + own.shape)
    got = lax.all_to_all(copies, "col", split_axis=0, concat_axis=0, tiled=True)
    parts = []
    for h in range(halves):
        src = []
        slot = []
        for c in range(mesh_cols):
            lower = c < mesh_cols // 2
            if h == 0:
                src.append(c if lower else mesh_cols - 1 - c)
            else:
                src.append(mesh_cols - 1 - c if lower else c)
            slot.append(0 if lower else 1)
        sel = got[np.array(src), :, :, np.array(slot), :]
        parts.append(sel.transpose(1, 2, 0, 3).reshape(2, half_pairs, mesh_cols * per_device))
    rows = jnp.concatenate(parts, axis=1)
    half = mesh_cols // 2
    send = lax.dynamic_slice_in_dim(rows, (col_pos // half) * half * per_device, half * per_device, 2)
    perm = []
    for src_r in range(mesh_rows):
        for src_c in range(mesh_cols):
            dst_r = src_c % half
            dst_c = 2 * src_r + src_c // half
            perm.append((src_r * mesh_cols + src_c, dst_r * mesh_cols + dst_c))
    cols = lax.ppermute(send, ("row", "col"), perm)

    val_hot = val_index[:, None] == jnp.arange(eps_val.shape[0], dtype=jnp.int32)[None, :]
    cond_hot = cond_index[:, None] == jnp.arange(eps_cond.shape[0], dtype=jnp.int32)[None, :]
    energy_v = jnp.sum(jnp.where(val_hot, eps_val[None, :], 0.0), axis=1)
    energy_c = jnp.sum(jnp.where(cond_hot, eps_cond[None, :], 0.0), axis=1)
    weight = (-6.0 / (math.sqrt(pairs) * (energy_c - energy_v)))[:, None]
    rows_re = rows[0]
    rows_im = rows[1]
    cols_re = cols[0]
    cols_im = cols[1]
    out_re = (
        chi0_in[0]
        + contract_pairs(weight * rows_re, cols_re)
        + contract_pairs(weight * rows_im, cols_im)
    )
    out_im = (
        chi0_in[1]
        + contract_pairs(weight * rows_im, cols_re)
        - contract_pairs(weight * rows_re, cols_im)
    )
    return jnp.stack([out_re, out_im])


def solution(mesh):
    return jax.shard_map(
        on_device,
        mesh=mesh,
        in_specs=(
            P(None, "row", "col", None),
            P(None, "row", "col", None),
            P(),
            P(),
            P(),
            P(),
            P(),
            P(None, "row", "col"),
        ),
        out_specs=P(None, "row", "col"),
        check_vma=False,
    )
```

profile of v0, /device:TPU:24, one launch (start us, length us, event | category | flops | bytes accessed | tf_op | source)
XLA Modules:
  0.0 566.9 jit_solution(6764291305822186480)
XLA Ops:
  2.1 4.4 fusion.117
  31.1 9.0 %select_multiply_fusion = (f32[128,4,8,128]{3,2,1,0:T(8,128)S(1)}, f32[128,4,8,128]{3,2,1,0:T(8,128)}, f32[128,4,8,128]{3,2,1,0:T(8,128)}, f32[128,4,8,128]{3,2,1,0:T(8,128)}) fusion(f32[128,4,8,128]{3,2,1,0:T(8,128)S(1)} %copy-done.3, f32[128,4,8,128]{3,2,1,0:T(8,128)} %gather_fusion.11, pred[128]{0:T(512)(128)(4,1)S(1)} %get-tuple-element.54, ...), kind=kLoop, calls=%fused_computation.49 | loop fusion | flops 6291456 | bytes 25166080 | tf_op jit(solution)/shard_map/mul | solution.py:77
  40.1 7.5 %fusion.14 = f32[2,8,9,2,64,4,8]{4,2,6,5,3,1,0:T(8,128)S(1)} fusion(f32[2,64,4,8,128,1,1]{4,3,2,1,0,6,5:T(8,128)S(1)} %bitcast.220, f32[1,128,8,9,2]{1,3,4,2,0:T(8,128)S(1)} %reverse_bitcast_fusion, f32[1,128,8,9,1]{1,3,4,2,0:T(8,128)S(1)} %get-tuple-element.41, f32[1,128,8,9,1]{1,3,4,2,0:T(8,128)S(1)} %get-tuple-element.40), kind=kOutput, calls=%fused_computation.38 | convolution fusion | flops 906043392 | bytes 4603904 | tf_op jit(solution)/shard_map/hpxyz,hzcjt->hcpxyjt/dot_general | solution.py:79
  47.7 4.3 copy.228
  52.0 5.9 %reshape.696 = f32[16,1,36864]{2,1,0:T(1,128)} reshape(f32[16,4,9,2,8,64]{5,4,3,2,1,0:T(8,128)} %bitcast.203) | data formatting | bytes 4718592
  57.9 7.8 %all-to-all-start.3 = ((f32[16,1,36864]{2,1,0:T(1,128)}), f32[16,1,36864]{2,1,0:T(1,128)S(1)}, u32[]{:S(2)}, u32[]{:S(2)}) async-start(f32[16,1,36864]{2,1,0:T(1,128)} %reshape.696), calls=%async_computation.3 | async-start | bytes 4718592 | tf_op jit(solution)/shard_map/all_to_all | solution.py:81
  65.7 9.1 %fusion.18 = f32[2,8,9,2,64,4,8]{4,2,6,5,3,1,0:T(8,128)S(1)} fusion(f32[2,64,4,8,128,1,1]{4,3,2,1,0,6,5:T(8,128)} %bitcast.219, f32[1,128,8,9,2]{1,3,4,2,0:T(8,128)S(1)} %reverse_bitcast_fusion, f32[1,128,8,9,1]{1,3,4,2,0:T(8,128)S(1)} %get-tuple-element.41, f32[1,128,8,9,1]{1,3,4,2,0:T(8,128)S(1)} %get-tuple-element.40), kind=kOutput, calls=%fused_computation.42 | convolution fusion | flops 906043392 | bytes 4603904 | tf_op jit(solution)/shard_map/hpxyz,hzcjt->hcpxyjt/dot_general | solution.py:79
  79.1 6.0 %reshape.692 = f32[16,1,36864]{2,1,0:T(1,128)} reshape(f32[16,4,9,2,8,64]{5,4,3,2,1,0:T(8,128)} %bitcast.204) | data formatting | bytes 4718592
  85.1 14.7 %all-to-all-done.3 = f32[16,1,36864]{2,1,0:T(1,128)S(1)} async-done(((f32[16,1,36864]{2,1,0:T(1,128)}), f32[16,1,36864]{2,1,0:T(1,128)S(1)}, u32[]{:S(2)}, u32[]{:S(2)}) %all-to-all-start.3) | async-done | bytes 2359328 | tf_op jit(solution)/shard_map/all_to_all | solution.py:81
  101.2 6.0 %all-to-all-start.1 = ((f32[16,1,36864]{2,1,0:T(1,128)}), f32[16,1,36864]{2,1,0:T(1,128)}, u32[]{:S(2)}, u32[]{:S(2)}) async-start(f32[16,1,36864]{2,1,0:T(1,128)} %reshape.692), calls=%async_computation.1 | async-start | bytes 4718592 | tf_op jit(solution)/shard_map/all_to_all | solution.py:81
  107.2 9.1 %fusion.16 = f32[2,8,9,2,64,4,8]{4,2,6,5,3,1,0:T(8,128)S(1)} fusion(f32[2,64,4,8,128,1,1]{4,3,2,1,0,6,5:T(8,128)} %bitcast.218, f32[1,128,8,9,2]{1,3,4,2,0:T(8,128)S(1)} %reverse_bitcast_fusion, f32[1,128,8,9,1]{1,3,4,2,0:T(8,128)S(1)} %get-tuple-element.41, f32[1,128,8,9,1]{1,3,4,2,0:T(8,128)S(1)} %get-tuple-element.40), kind=kOutput, calls=%fused_computation.40 | convolution fusion | flops 906043392 | bytes 4603904 | tf_op jit(solution)/shard_map/hpxyz,hzcjt->hcpxyjt/dot_general | solution.py:79
  120.6 5.9 %reshape.694 = f32[16,1,36864]{2,1,0:T(1,128)} reshape(f32[16,4,9,2,8,64]{5,4,3,2,1,0:T(8,128)} %bitcast.205) | data formatting | bytes 4718592
  126.5 12.5 %all-to-all-done.1 = f32[16,1,36864]{2,1,0:T(1,128)} async-done(((f32[16,1,36864]{2,1,0:T(1,128)}), f32[16,1,36864]{2,1,0:T(1,128)}, u32[]{:S(2)}, u32[]{:S(2)}) %all-to-all-start.1) | async-done | bytes 2359328 | tf_op jit(solution)/shard_map/all_to_all | solution.py:81
  139.1 5.3 all-to-all-start.2
  144.6 9.1 %fusion.20 = f32[2,8,9,2,64,4,8]{4,2,6,5,3,1,0:T(8,128)S(1)} fusion(f32[2,64,4,8,128,1,1]{4,3,2,1,0,6,5:T(8,128)} %bitcast.217, f32[1,128,8,9,2]{1,3,4,2,0:T(8,128)S(1)} %reverse_bitcast_fusion, f32[1,128,8,9,1]{1,3,4,2,0:T(8,128)S(1)} %get-tuple-element.41, f32[1,128,8,9,1]{1,3,4,2,0:T(8,128)S(1)} %get-tuple-element.40), kind=kOutput, calls=%fused_computation.44 | convolution fusion | flops 906043392 | bytes 4603904 | tf_op jit(solution)/shard_map/hpxyz,hzcjt->hcpxyjt/dot_general | solution.py:79
  158.0 5.9 %reshape.690 = f32[16,1,36864]{2,1,0:T(1,128)} reshape(f32[16,4,9,2,8,64]{5,4,3,2,1,0:T(8,128)} %bitcast.206) | data formatting | bytes 4718592
  164.5 12.7 %all-to-all-done.2 = f32[16,1,36864]{2,1,0:T(1,128)S(1)} async-done(((f32[16,1,36864]{2,1,0:T(1,128)}), f32[16,1,36864]{2,1,0:T(1,128)S(1)}, u32[]{:S(2)}, u32[]{:S(2)}) %all-to-all-start.2) | async-done | bytes 2359328 | tf_op jit(solution)/shard_map/all_to_all | solution.py:81
  178.6 6.4 %all-to-all-start = ((f32[16,1,36864]{2,1,0:T(1,128)}), f32[16,1,36864]{2,1,0:T(1,128)}, u32[]{:S(2)}, u32[]{:S(2)}) async-start(f32[16,1,36864]{2,1,0:T(1,128)} %reshape.690), calls=%async_computation | async-start | bytes 4718592 | tf_op jit(solution)/shard_map/all_to_all | solution.py:81
  191.6 8.0 %reduce = f32[16,36864]{1,0:T(8,128)S(1)} reduce(f32[16,1,36864]{2,1,0:T(1,128)} %copy-done.1, f32[]{:T(128)} %broadcast.768), dimensions={1}, to_apply=%all_to_all.21.reduce_sub_computation | reduce | bytes 4718596 | tf_op jit(solution)/shard_map/all_to_all | solution.py:81
  203.0 11.5 %fusion.33 = f32[64,4,128,9,2]{2,0,3,1,4:T(8,128)S(1)} fusion(f32[16,64,4,8,9,2]{1,3,5,4,2,0:T(8,128)} %bitcast.208, f32[16,8,1,128,1]{3,0,1,2,4:T(8,128)S(1)} %get-tuple-element.39, f32[16,8,1,128,1]{3,0,1,2,4:T(8,128)S(1)} %get-tuple-element.38, f32[16,8,1,128,1]{3,0,1,2,4:T(8,128)S(1)} %get-tuple-element.37), kind=kOutput, calls=%fused_computation.64 | convolution fusion | flops 1812135936 | bytes 4915200 | tf_op jit(solution)/shard_map/spxyjt,syteu->pxeju/dot_general | solution.py:82
  214.5 5.0 copy.164
  219.5 8.1 %copy.165 = f32[64,4,1152,2]{0,1,3,2:T(4,128)} copy(f32[64,4,1152,2]{0,3,2,1:T(2,128)} %bitcast.209) | data formatting | bytes 4718592 | tf_op jit(solution)/shard_map/reshape | solution.py:83
  227.6 8.0 %reduce.1 = f32[16,36864]{1,0:T(8,128)S(1)} reduce(f32[16,1,36864]{2,1,0:T(1,128)} %all-to-all-done.1, f32[]{:T(128)} %broadcast.768), dimensions={1}, to_apply=%all_to_all.19.reduce_sub_computation | reduce | bytes 4718596 | tf_op jit(solution)/shard_map/all_to_all | solution.py:81
  239.4 11.5 %fusion.27 = f32[64,4,128,9,2]{2,0,3,1,4:T(8,128)S(1)} fusion(f32[16,64,4,8,9,2]{1,3,5,4,2,0:T(8,128)} %bitcast.210, f32[16,8,1,128,1]{3,0,1,2,4:T(8,128)S(1)} %get-tuple-element.39, f32[16,8,1,128,1]{3,0,1,2,4:T(8,128)S(1)} %get-tuple-element.38, f32[16,8,1,128,1]{3,0,1,2,4:T(8,128)S(1)} %get-tuple-element.37), kind=kOutput, calls=%fused_computation.62 | convolution fusion | flops 1812135936 | bytes 4915200 | tf_op jit(solution)/shard_map/spxyjt,syteu->pxeju/dot_general | solution.py:82
  250.9 4.9 copy.144
  255.8 8.0 %copy.145 = f32[64,4,1152,2]{0,1,3,2:T(4,128)} copy(f32[64,4,1152,2]{0,3,2,1:T(2,128)} %bitcast.211) | data formatting | bytes 4718592 | tf_op jit(solution)/shard_map/reshape | solution.py:83
  263.8 11.8 %gather_fusion.13 = f32[1024,64,4,2]{1,2,3,0:T(4,128)} fusion(f32[64,4,1152,2]{0,1,3,2:T(4,128)} %copy.165, s32[1024]{0:T(1024)S(1)} %broadcast_clamp_fusion), kind=kCustom, calls=%fused_computation.11.clone | custom fusion | bytes 4198400 | tf_op jit(solution)/shard_map/jit(_take)/gather | solution.py:84
  275.6 12.1 %gather_fusion.7 = f32[1024,64,4,2]{1,2,3,0:T(4,128)} fusion(f32[64,4,1152,2]{0,1,3,2:T(4,128)} %copy.145, s32[1024]{0:T(1024)S(1)} %broadcast_clamp_fusion), kind=kCustom, calls=%fused_computation.9.clone | custom fusion | bytes 4198400 | tf_op jit(solution)/shard_map/jit(_take)/gather | solution.py:84
  287.7 8.0 %reduce.2 = f32[16,36864]{1,0:T(8,128)S(1)} reduce(f32[16,1,36864]{2,1,0:T(1,128)} %copy-done.2, f32[]{:T(128)} %broadcast.768), dimensions={1}, to_apply=%all_to_all.20.reduce_sub_computation | reduce | bytes 4718596 | tf_op jit(solution)/shard_map/all_to_all | solution.py:81
  299.2 11.5 %fusion.30 = f32[64,4,128,9,2]{2,0,3,1,4:T(8,128)S(1)} fusion(f32[16,64,4,8,9,2]{1,3,5,4,2,0:T(8,128)} %bitcast.212, f32[16,8,1,128,1]{3,0,1,2,4:T(8,128)S(1)} %copy-done.11, f32[16,8,1,128,1]{3,0,1,2,4:T(8,128)S(1)} %copy-done.9, f32[16,8,1,128,1]{3,0,1,2,4:T(8,128)S(1)} %copy-done.7), kind=kOutput, calls=%fused_computation.63 | convolution fusion | flops 1812135936 | bytes 4915200 | tf_op jit(solution)/shard_map/spxyjt,syteu->pxeju/dot_general | solution.py:82
  310.7 5.0 copy.154
  315.7 8.0 %copy.155 = f32[64,4,1152,2]{0,1,3,2:T(4,128)} copy(f32[64,4,1152,2]{0,3,2,1:T(2,128)} %bitcast.213) | data formatting | bytes 4718592 | tf_op jit(solution)/shard_map/reshape | solution.py:83
  323.6 12.3 %gather_fusion.10 = f32[1024,64,4,2]{1,2,3,0:T(4,128)} fusion(f32[64,4,1152,2]{0,1,3,2:T(4,128)} %copy.155, s32[1024]{0:T(1024)S(1)} %broadcast_clamp_fusion), kind=kCustom, calls=%fused_computation.10.clone | custom fusion | bytes 4198400 | tf_op jit(solution)/shard_map/jit(_take)/gather | solution.py:84
  335.9 8.0 %reduce.3 = f32[16,36864]{1,0:T(8,128)S(1)} reduce(f32[16,1,36864]{2,1,0:T(1,128)} %all-to-all-done, f32[]{:T(128)} %broadcast.768), dimensions={1}, to_apply=%all_to_all.18.reduce_sub_computation | reduce | bytes 4718596 | tf_op jit(solution)/shard_map/all_to_all | solution.py:81
  347.4 11.5 %fusion.24 = f32[64,4,128,9,2]{2,0,3,1,4:T(8,128)S(1)} fusion(f32[16,64,4,8,9,2]{1,3,5,4,2,0:T(8,128)} %bitcast.207, f32[16,8,1,128,1]{3,0,1,2,4:T(8,128)S(1)} %copy-done.11, f32[16,8,1,128,1]{3,0,1,2,4:T(8,128)S(1)} %copy-done.9, f32[16,8,1,128,1]{3,0,1,2,4:T(8,128)S(1)} %copy-done.7), kind=kOutput, calls=%fused_computation.61 | convolution fusion | flops 1812135936 | bytes 4915200 | tf_op jit(solution)/shard_map/spxyjt,syteu->pxeju/dot_general | solution.py:82
  358.9 5.0 copy.134
  363.8 8.0 %copy.135 = f32[64,4,1152,2]{0,1,3,2:T(4,128)} copy(f32[64,4,1152,2]{0,3,2,1:T(2,128)} %bitcast.214) | data formatting | bytes 4718592 | tf_op jit(solution)/shard_map/reshape | solution.py:83
  371.8 12.0 %gather_fusion.4 = f32[1024,64,4,2]{1,2,3,0:T(4,128)} fusion(f32[64,4,1152,2]{0,1,3,2:T(4,128)} %copy.135, s32[1024]{0:T(1024)S(1)} %broadcast_clamp_fusion), kind=kCustom, calls=%fused_computation.1.clone | custom fusion | bytes 4198400 | tf_op jit(solution)/shard_map/jit(_take)/gather | solution.py:84
  383.8 13.9 %select_bitcast_fusion = (f32[64,4,1024,2]{0,1,3,2:T(4,128)}, f32[64,4,1024,2]{0,1,3,2:T(4,128)}, f32[64,4,1024,2]{0,1,3,2:T(4,128)}, f32[64,4,1024,2]{0,1,3,2:T(4,128)S(1)}) fusion(f32[1024,64,4,2]{1,2,3,0:T(4,128)} %gather_fusion.13, pred[1024]{0:T(1024)(128)(4,1)S(1)} %copy-done.18, f32[1024,64,4,2]{1,2,3,0:T(4,128)} %gather_fusion.7, ...), kind=kLoop, calls=%fused_computation.27 | loop fusion | flops 2097152 | bytes 16778240 | tf_op jit(solution)/shard_map/jit(_take)/select_n | solution.py:84
  401.7 8.1 %add_reduce_fusion.3 = (f32[64,1024]{0,1:T(8,128)S(1)}, f32[64,1024]{0,1:T(8,128)S(1)}) fusion(f32[64,4,1024]{0,1,2:T(4,128)S(1)} %copy.137, f32[64,4,1024,2]{0,1,3,2:T(4,128)} %copy-done, f32[4,1024]{0,1:T(8,128)} %get-tuple-element.56, f32[4,1024]{0,1:T(8,128)} %get-tuple-element.28), kind=kLoop, calls=%fused_computation.60 | loop fusion | flops 1966080 | bytes 2654208 | tf_op jit(solution)/shard_map/reduce_sum | solution.py:89
  414.4 8.1 %add_reduce_fusion.2 = (f32[64,1024]{0,1:T(8,128)S(1)}, f32[64,1024]{0,1:T(8,128)S(1)}) fusion(f32[64,4,1024]{0,1,2:T(4,128)S(1)} %copy.147, f32[64,4,1024,2]{0,1,3,2:T(4,128)} %get-tuple-element.45, f32[4,1024]{0,1:T(8,128)} %get-tuple-element.57, f32[4,1024]{0,1:T(8,128)} %get-tuple-element.27), kind=kLoop, calls=%fused_computation.58 | loop fusion | flops 1966080 | bytes 2654208 | tf_op jit(solution)/shard_map/reduce_sum | solution.py:89
  427.8 8.1 %add_reduce_fusion.1 = (f32[64,1024]{0,1:T(8,128)S(1)}, f32[64,1024]{0,1:T(8,128)S(1)}) fusion(f32[64,4,1024]{0,1,2:T(4,128)S(1)} %copy.157, f32[64,4,1024,2]{0,1,3,2:T(4,128)} %get-tuple-element.46, f32[4,1024]{0,1:T(8,128)} %get-tuple-element.58, f32[4,1024]{0,1:T(8,128)} %get-tuple-element.26), kind=kLoop, calls=%fused_computation.56 | loop fusion | flops 1966080 | bytes 2654208 | tf_op jit(solution)/shard_map/reduce_sum | solution.py:89
  441.1 8.1 %add_reduce_fusion = (f32[64,1024]{0,1:T(8,128)S(1)}, f32[64,1024]{0,1:T(8,128)S(1)}) fusion(f32[64,4,1024]{0,1,2:T(4,128)S(1)} %copy.167, f32[64,4,1024,2]{0,1,3,2:T(4,128)} %get-tuple-element.44, f32[4,1024]{0,1:T(8,128)} %get-tuple-element.59, f32[4,1024]{0,1:T(8,128)} %get-tuple-element.25), kind=kLoop, calls=%fused_computation.54 | loop fusion | flops 1966080 | bytes 2654208 | tf_op jit(solution)/shard_map/reduce_sum | solution.py:89
  451.1 15.9 %all_to_all.30 = f32[8,2,64,128]{3,2,1,0:T(8,128)S(1)} all-to-all(f32[8,2,64,128]{3,2,1,0:T(8,128)S(1)} %fusion.45), channel_id=1, replica_groups=mesh['row'=8,'col'=16] {'row'}, dimensions={0} | all-to-all | bytes 1048576 | tf_op jit(solution)/shard_map/all_to_all | solution.py:96
  469.8 7.2 %all-to-all-start.5 = ((f32[16,1,16384]{2,1,0:T(1,128)}), f32[16,1,16384]{2,1,0:T(1,128)S(1)}, u32[]{:S(2)}, u32[]{:S(2)}) async-start(f32[16,1,16384]{2,1,0:T(1,128)} %reshape.698), calls=%async_computation.5 | async-start | bytes 2097152 | tf_op jit(solution)/shard_map/all_to_all | solution.py:99
  477.0 14.5 %all-to-all-done.5 = f32[16,1,16384]{2,1,0:T(1,128)S(1)} async-done(((f32[16,1,16384]{2,1,0:T(1,128)}), f32[16,1,16384]{2,1,0:T(1,128)S(1)}, u32[]{:S(2)}, u32[]{:S(2)}) %all-to-all-start.5) | async-done | bytes 1048608 | tf_op jit(solution)/shard_map/all_to_all | solution.py:99
  505.0 4.7 collective-permute-start
  509.9 46.3 %collective-permute-done = f32[2,128,512]{2,1,0:T(8,128)S(1)} collective-permute-done((f32[2,128,512]{2,1,0:T(8,128)S(1)}, f32[2,128,512]{2,1,0:T(8,128)S(1)}, u32[]{:S(2)}, u32[]{:S(2)}) %collective-permute-start) | collective-permute-done | bytes 524320 | tf_op jit(solution)/shard_map/ppermute | solution.py:122
  (128 shorter events, 111.5 us)
Async XLA Ops:
  2.1 4.4 copy-start.5
  28.9 2.2 copy-start.3
  57.9 41.9 %all-to-all-start.3 = ((f32[16,1,36864]{2,1,0:T(1,128)}), f32[16,1,36864]{2,1,0:T(1,128)S(1)}, u32[]{:S(2)}, u32[]{:S(2)}) async-start(f32[16,1,36864]{2,1,0:T(1,128)} %reshape.696), calls=%async_computation.3 | async-start | bytes 4718592 | tf_op jit(solution)/shard_map/all_to_all | solution.py:81
  99.8 1.4 copy-start.1
  101.2 37.9 %all-to-all-start.1 = ((f32[16,1,36864]{2,1,0:T(1,128)}), f32[16,1,36864]{2,1,0:T(1,128)}, u32[]{:S(2)}, u32[]{:S(2)}) async-start(f32[16,1,36864]{2,1,0:T(1,128)} %reshape.692), calls=%async_computation.1 | async-start | bytes 4718592 | tf_op jit(solution)/shard_map/all_to_all | solution.py:81
  126.5 17.9 %copy-start.15 = (s32[8192]{0:T(1024)S(1)}, s32[8192]{0:T(1024)}, u32[]{:S(2)}) copy-start(s32[8192]{0:T(1024)} %param.26) | copy-start | bytes 98308
  139.1 38.2 %all-to-all-start.2 = ((f32[16,1,36864]{2,1,0:T(1,128)}), f32[16,1,36864]{2,1,0:T(1,128)S(1)}, u32[]{:S(2)}, u32[]{:S(2)}) async-start(f32[16,1,36864]{2,1,0:T(1,128)} %reshape.694), calls=%async_computation.2 | async-start | bytes 4718592 | tf_op jit(solution)/shard_map/all_to_all | solution.py:81
  177.2 1.4 copy-start.2
  178.6 157.3 %all-to-all-start = ((f32[16,1,36864]{2,1,0:T(1,128)}), f32[16,1,36864]{2,1,0:T(1,128)}, u32[]{:S(2)}, u32[]{:S(2)}) async-start(f32[16,1,36864]{2,1,0:T(1,128)} %reshape.690), calls=%async_computation | async-start | bytes 4718592 | tf_op jit(solution)/shard_map/all_to_all | solution.py:81
  186.0 53.3 %copy-start.6 = (f32[16,8,1,128,1]{3,0,1,2,4:T(8,128)}, f32[16,8,1,128,1]{3,0,1,2,4:T(8,128)S(1)}, u32[]{:S(2)}) copy-start(f32[16,8,1,128,1]{3,0,1,2,4:T(8,128)S(1)} %get-tuple-element.37) | copy-start | bytes 196612
  186.0 53.3 %copy-start.8 = (f32[16,8,1,128,1]{3,0,1,2,4:T(8,128)}, f32[16,8,1,128,1]{3,0,1,2,4:T(8,128)S(1)}, u32[]{:S(2)}) copy-start(f32[16,8,1,128,1]{3,0,1,2,4:T(8,128)S(1)} %get-tuple-element.38) | copy-start | bytes 196612
  186.0 53.3 %copy-start.10 = (f32[16,8,1,128,1]{3,0,1,2,4:T(8,128)}, f32[16,8,1,128,1]{3,0,1,2,4:T(8,128)S(1)}, u32[]{:S(2)}) copy-start(f32[16,8,1,128,1]{3,0,1,2,4:T(8,128)S(1)} %get-tuple-element.39) | copy-start | bytes 196612
  295.7 3.6 copy-start.7
  295.7 3.6 copy-start.9
  295.7 3.6 copy-start.11
  371.8 12.0 %copy-start.18 = (pred[1024]{0:T(1024)(128)(4,1)S(1)}, pred[1024]{0:T(1024)(128)(4,1)}, u32[]{:S(2)}) copy-start(pred[1024]{0:T(1024)(128)(4,1)} %get-tuple-element.15) | copy-start | bytes 3076
  397.7 1.9 copy-start
  441.1 8.5 %copy-start.14 = (f32[2,8,128]{2,0,1:T(2,128)S(1)}, f32[2,8,128]{2,0,1:T(2,128)}, u32[]{:S(2)}) copy-start(f32[2,8,128]{2,0,1:T(2,128)} %pad_bitcast_fusion) | copy-start | bytes 24580
  469.8 21.7 %all-to-all-start.5 = ((f32[16,1,16384]{2,1,0:T(1,128)}), f32[16,1,16384]{2,1,0:T(1,128)S(1)}, u32[]{:S(2)}, u32[]{:S(2)}) async-start(f32[16,1,16384]{2,1,0:T(1,128)} %reshape.698), calls=%async_computation.5 | async-start | bytes 2097152 | tf_op jit(solution)/shard_map/all_to_all | solution.py:99
  494.6 0.9 copy-start.13
  496.1 5.0 copy-start.12
  504.5 5.2 copy-start.16
  504.6 5.2 copy-start.17
  504.6 5.2 copy-start.19
  504.6 5.2 copy-start.20
  505.0 51.2 %collective-permute-start = (f32[2,128,512]{2,1,0:T(8,128)S(1)}, f32[2,128,512]{2,1,0:T(8,128)S(1)}, u32[]{:S(2)}, u32[]{:S(2)}) collective-permute-start(f32[2,128,512]{2,1,0:T(8,128)S(1)} %constant_dynamic-slice_fusion), channel_id=1, source_target_pairs={{0,0},{1,16},{2,32},{3,48},{4,64},{5,80},{6,96},{7,112},{8,1},{9,1... | collective-permute-start | bytes 1572872 | tf_op jit(solution)/shard_map/ppermute | solution.py:122
  556.2 3.8 copy-start.4
where the time goes:
time: 572 us; the launch traced here: 567 us
  local copies, waits for them, and re-layouts  223 us (39%)
  waiting for transfers between devices  101 us (18%)
  other arithmetic  99.7 us (17%)
  matrix products  88.8 us (16%)
  starting transfers between devices  37.4 us (7%)
  blocking collectives  15.9 us (3%)
    gather x4, local copies, waits for them, and re-layouts, on_device(): chosen = jnp.take(flat, pick, axis=2)  48.2 us
    unnamed x54, local copies, waits for them, and re-layouts  47.1 us
    ppermute x1, waiting for transfers between devices, on_device(): cols = lax.ppermute(send, ('row', 'col'), perm)  46.3 us
    dot_general x4, matrix products, on_device(): y_all = jnp.einsum('spxyjt,syteu->pxeju', z_mine, table_y, precision=HIGH)  46 us
    all_to_all x4, waiting for transfers between devices, on_device(): lax.all_to_all(z_all, 'col', split_axis=0, concat_axis=0, tiled=True)  39.9 us
    dot_general x4, matrix products, on_device(): z_all = jnp.einsum('hpxyz,hzcjt->hcpxyjt', rho, table_z, precision=HIGH)  34.8 us
    reduce_sum x4, other arithmetic, on_device(): part_re = jnp.sum(c_re * cx[None] + c_im * sx[None], axis=1)  32.5 us
    reshape x4, local copies, waits for them, and re-layouts, on_device(): flat = y_all.reshape(half_pairs, chunk, GRID * span_z, 2)  32 us
  transfers between devices with their start and end apart: 6, of which 5 were waited for; matrix products, arithmetic and copies ran while one was open for 37% of the time, Pallas kernels for 0%

commit v1 on v0

--- a/solution.py
+++ b/solution.py
@@ -37,12 +37,11 @@
     col_span = GRID // mesh_cols
     steps = jnp.arange(GRID, dtype=jnp.int32)
 
-    halves = 2
-    half_pairs = pairs // halves
     mirror = mesh_cols - 1 - col_pos
     low = jnp.minimum(col_pos, mirror)
     side = col_pos // (mesh_cols // 2)
     span_z = col_span + 1
+    x_half = row_span // 2
     by_block = gmap.reshape(mesh_rows, mesh_cols, per_device)
     direct = lax.dynamic_index_in_dim(by_block, low, axis=1, keepdims=False)
     mirrored = lax.dynamic_index_in_dim(by_block, mesh_cols - 1 - low, axis=1, keepdims=False)
@@ -56,7 +55,7 @@
     freq_z = jnp.where(flip == 1, (GRID - freq_z) % GRID, freq_z) - low * col_span
     sign = jnp.where(flip == 1, -1.0, 1.0).astype(jnp.float32)
     pick = freq_y * span_z + freq_z
-    x_glob = row_pos * row_span + jnp.arange(row_span, dtype=jnp.int32)
+    x_glob = row_pos * row_span + side * x_half + jnp.arange(x_half, dtype=jnp.int32)
     cos_x, sin_x = phase_table(x_glob, freq_x, GRID)
 
     kz_set = (jnp.arange(mesh_cols // 2, dtype=jnp.int32)[:, None] * col_span
@@ -70,47 +69,40 @@
     ).reshape(mesh_cols, col_span, 2, GRID, 2)
 
     chunks = 4
-    chunk = row_span // chunks
+    chunk = x_half // chunks
     partial = None
     for i in range(chunks):
-        xs = slice(i * chunk, (i + 1) * chunk)
-        rho = jnp.take(psi_val[:, xs], val_index, axis=0) * jnp.take(psi_cond[:, xs], cond_index, axis=0)
-        rho = rho.reshape((halves, half_pairs) + rho.shape[1:])
-        z_all = jnp.einsum("hpxyz,hzcjt->hcpxyjt", rho, table_z, precision=HIGH)
+        lo = slice(i * chunk, (i + 1) * chunk)
+        hi = slice(x_half + i * chunk, x_half + (i + 1) * chunk)
+        band_v = jnp.stack([psi_val[:, lo], psi_val[:, hi]], axis=1)
+        band_c = jnp.stack([psi_cond[:, lo], psi_cond[:, hi]], axis=1)
+        rho = jnp.take(band_v, val_index, axis=0) * jnp.take(band_c, cond_index, axis=0)
+        z_all = jnp.einsum("phxyz,hzcjt->hcpxyjt", rho, table_z, precision=HIGH)
         z_all = z_all.reshape((mesh_cols,) + z_all.shape[2:])
         z_mine = lax.all_to_all(z_all, "col", split_axis=0, concat_axis=0, tiled=True)
         y_all = jnp.einsum("spxyjt,syteu->pxeju", z_mine, table_y, precision=HIGH)
-        flat = y_all.reshape(half_pairs, chunk, GRID * span_z, 2)
+        flat = y_all.reshape(pairs, chunk, GRID * span_z, 2)
         chosen = jnp.take(flat, pick, axis=2)
         c_re = chosen[..., 0]
         c_im = chosen[..., 1]
-        cx = cos_x[xs]
-        sx = sin_x[xs]
+        cx = cos_x[lo]
+        sx = sin_x[lo]
         part_re = jnp.sum(c_re * cx[None] + c_im * sx[None], axis=1)
         part_im = jnp.sum(c_im * cx[None] - c_re * sx[None], axis=1)
         piece = jnp.stack([part_re, part_im], axis=0)
         partial = piece if partial is None else partial + piece
     partial = partial * jnp.stack([jnp.ones_like(sign), sign])[:, None, :] * scale
     block = 2 * per_device
-    spread = partial.reshape(2, half_pairs, mesh_rows, block).transpose(2, 0, 1, 3)
+    spread = partial.reshape(2, pairs, mesh_rows, block).transpose(2, 0, 1, 3)
     gathered = lax.all_to_all(spread, "row", split_axis=0, concat_axis=0, tiled=True)
-    own = jnp.sum(gathered, axis=0).reshape(2, half_pairs, 2, per_device)
+    both_blocks = jnp.sum(gathered, axis=0).reshape(2, pairs, 2, per_device)
+    mine = lax.dynamic_index_in_dim(both_blocks, side, axis=2, keepdims=False)
+    theirs = lax.dynamic_index_in_dim(both_blocks, 1 - side, axis=2, keepdims=False)
+    partner = lax.ppermute(theirs, "col", [(c, mesh_cols - 1 - c) for c in range(mesh_cols)])
+    own = mine + partner
     copies = jnp.broadcast_to(own[None], (mesh_cols,) + own.shape)
-    got = lax.all_to_all(copies, "col", split_axis=0, concat_axis=0, tiled=True)
-    parts = []
-    for h in range(halves):
-        src = []
-        slot = []
-        for c in range(mesh_cols):
-            lower = c < mesh_cols // 2
-            if h == 0:
-                src.append(c if lower else mesh_cols - 1 - c)
-            else:
-                src.append(mesh_cols - 1 - c if lower else c)
-            slot.append(0 if lower else 1)
-        sel = got[np.array(src), :, :, np.array(slot), :]
-        parts.append(sel.transpose(1, 2, 0, 3).reshape(2, half_pairs, mesh_cols * per_device))
-    rows = jnp.concatenate(parts, axis=1)
+    row_blocks = lax.all_to_all(copies, "col", split_axis=0, concat_axis=0, tiled=True)
+    rows = row_blocks.transpose(1, 2, 0, 3).reshape(2, pairs, mesh_cols * per_device)
     half = mesh_cols // 2
     send = lax.dynamic_slice_in_dim(rows, (col_pos // half) * half * per_device, half * per_device, 2)
     perm = []

time: 572 us -> 452 us (0.79)
  local copies, waits for them, and re-layouts: 223 us -> 121 us
  waiting for transfers between devices: 101 us -> 152 us
  matrix products: 88.8 us -> 49.8 us
  other arithmetic: 99.7 us -> 70.3 us
  starting transfers between devices: 37.4 us -> 55.9 us
  blocking collectives: 15.9 us -> 0 us
    unnamed x54, local copies, waits for them, and re-layouts: 47.1 us -> 2 us
    all_to_all x5 -> x0, other arithmetic: 35 us -> none  [the longest x4 31.8 us: on_device(): lax.all_to_all(z_all, 'col', split_axis=0, concat_axis=0, tiled=True)]
    reshape x6 -> x0, local copies, waits for them, and re-layouts: 34.7 us -> none  [the longest x4 32 us: on_device(): flat = y_all.reshape(half_pairs, chunk, GRID * span_z, 2)]
    all_to_all x4, waiting for transfers between devices: 39.9 us -> 71.3 us  [on_device(): lax.all_to_all(z_all, 'col', split_axis=0, concat_axis=0, tiled=True)]
    dot_general x4, matrix products: 46 us -> 19.2 us  [on_device(): y_all = jnp.einsum('spxyjt,syteu->pxeju', z_mine, table_y, precision=HIGH)]
    all_to_all x1 -> x0, blocking collectives: 15.9 us -> none  [on_device(): lax.all_to_all(spread, 'row', split_axis=0, concat_axis=0, tiled=True)]
    all_to_all x1 -> x2, waiting for transfers between devices: 14.5 us -> 29.5 us  [the longest x1 16 us: on_device(): lax.all_to_all(spread, 'row', split_axis=0, concat_axis=0, tiled=True)]
    dot_general x4, matrix products: 34.8 us -> 22.9 us  [on_device(): z_all = jnp.einsum('phxyz,hzcjt->hcpxyjt', rho, table_z, precision=HIGH)]
  transfers between devices with their start and end apart: 6 -> 8, of which waited for: 5 -> 7; matrix products, arithmetic and copies ran while one was open for 37% -> 18% of each run, Pallas kernels for 0% -> 0%
where the time goes in v1:
time: 452 us; the launch traced here: 450 us
  waiting for transfers between devices  152 us (34%)
  local copies, waits for them, and re-layouts  121 us (27%)
  other arithmetic  70.3 us (16%)
  starting transfers between devices  55.9 us (12%)
  matrix products  49.8 us (11%)
    all_to_all x4, waiting for transfers between devices, on_device(): lax.all_to_all(z_all, 'col', split_axis=0, concat_axis=0, tiled=True)  71.3 us
    ppermute x1, waiting for transfers between devices, on_device(): cols = lax.ppermute(send, ('row', 'col'), perm)  45.8 us
    gather x4, local copies, waits for them, and re-layouts, on_device(): chosen = jnp.take(flat, pick, axis=2)  40.7 us
    reduce_sum x4, other arithmetic, on_device(): part_re = jnp.sum(c_re * cx[None] + c_im * sx[None], axis=1)  37.2 us
    all_to_all x4, starting transfers between devices, on_device(): lax.all_to_all(z_all, 'col', split_axis=0, concat_axis=0, tiled=True)  36.6 us
    dot_general x4, matrix products, on_device(): z_all = jnp.einsum('phxyz,hzcjt->hcpxyjt', rho, table_z, precision=HIGH)  22.9 us
    dot_general x4, matrix products, on_device(): y_all = jnp.einsum('spxyjt,syteu->pxeju', z_mine, table_y, precision=HIGH)  19.2 us
    all_to_all x1, waiting for transfers between devices, on_device(): lax.all_to_all(spread, 'row', split_axis=0, concat_axis=0, tiled=True)  16 us
  transfers between devices with their start and end apart: 8, of which 7 were waited for; matrix products, arithmetic and copies ran while one was open for 18% of the time, Pallas kernels for 0%

profile of v1, /device:TPU:24, one launch (start us, length us, event | category | flops | bytes accessed | tf_op | source)
XLA Modules:
  0.0 449.8 jit_solution(7112582275722941324)
XLA Ops:
  2.1 3.8 slice_bitcast_fusion.3
  28.8 8.7 %fusion.24 = (f32[128,2,2,8,128,1,1]{4,3,2,1,0,6,5:T(8,128)}, f32[128,2,2,8,128,1,1]{4,3,2,1,0,6,5:T(8,128)}, f32[128,2,2,8,128,1,1]{4,3,2,1,0,6,5:T(8,128)}, f32[128,2,2,8,128,1,1]{4,3,2,1,0,6,5:T(8,128)S(1)}) fusion(f32[128,2,2,8,128]{4,3,2,1,0:T(8,128)} %gather_fusion.10, f32[128,2,2,8,128]{4,3,2,1,0:T(8,128)} %gather_fusion.9, ...), kind=kLoop, calls=%fused_computation.41 | loop fusion | flops 6291456 | bytes 25166080 | tf_op jit(solution)/shard_map/mul | solution.py:79
  37.5 4.6 %fusion.20 = f32[2,8,9,2,128,2,8]{4,2,6,5,3,1,0:T(8,128)S(1)} fusion(f32[128,2,2,8,128,1,1]{4,3,2,1,0,6,5:T(8,128)S(1)} %get-tuple-element.71, f32[1,128,8,9,2]{1,3,4,2,0:T(8,128)S(1)} %reverse_bitcast_fusion, f32[1,128,8,9,1]{1,3,4,2,0:T(8,128)S(1)} %get-tuple-element.61, f32[1,128,8,9,1]{1,3,4,2,0:T(8,128)S(1)} %get-tuple-element.60), kind=kOutput, calls=%fused_computation.34 | convolution fusion | flops 906043392 | bytes 4603904 | tf_op jit(solution)/shard_map/phxyz,hzcjt->hcpxyjt/dot_general | solution.py:80
  42.0 2.4 copy.121
  44.4 19.1 %all-to-all-start = ((f32[16,128,2,8,9,2]{1,3,5,4,2,0:T(8,128)}), f32[16,128,2,8,9,2]{1,3,5,4,2,0:T(8,128)S(1)}, u32[]{:S(2)}, u32[]{:S(2)}) async-start(f32[16,128,2,8,9,2]{1,3,5,4,2,0:T(8,128)} %copy.121), calls=%async_computation | async-start | bytes 4718592 | tf_op jit(solution)/shard_map/all_to_all | solution.py:82
  63.5 6.1 %fusion.18 = f32[2,8,9,2,128,2,8]{4,2,6,5,3,1,0:T(8,128)S(1)} fusion(f32[128,2,2,8,128,1,1]{4,3,2,1,0,6,5:T(8,128)} %get-tuple-element.69, f32[1,128,8,9,2]{1,3,4,2,0:T(8,128)S(1)} %reverse_bitcast_fusion, f32[1,128,8,9,1]{1,3,4,2,0:T(8,128)S(1)} %get-tuple-element.61, f32[1,128,8,9,1]{1,3,4,2,0:T(8,128)S(1)} %get-tuple-element.60), kind=kOutput, calls=%fused_computation.32 | convolution fusion | flops 906043392 | bytes 4603904 | tf_op jit(solution)/shard_map/phxyz,hzcjt->hcpxyjt/dot_general | solution.py:80
  69.6 2.4 copy.130
  72.0 25.6 %all-to-all-done = f32[16,128,2,8,9,2]{1,3,5,4,2,0:T(8,128)S(1)} async-done(((f32[16,128,2,8,9,2]{1,3,5,4,2,0:T(8,128)}), f32[16,128,2,8,9,2]{1,3,5,4,2,0:T(8,128)S(1)}, u32[]{:S(2)}, u32[]{:S(2)}) %all-to-all-start) | async-done | bytes 2359328 | tf_op jit(solution)/shard_map/all_to_all | solution.py:82
  97.6 5.7 %all-to-all-start.1 = ((f32[16,128,2,8,9,2]{1,3,5,4,2,0:T(8,128)}), f32[16,128,2,8,9,2]{1,3,5,4,2,0:T(8,128)}, u32[]{:S(2)}, u32[]{:S(2)}) async-start(f32[16,128,2,8,9,2]{1,3,5,4,2,0:T(8,128)} %copy.130), calls=%async_computation.1 | async-start | bytes 4718592 | tf_op jit(solution)/shard_map/all_to_all | solution.py:82
  103.3 6.1 %fusion.16 = f32[2,8,9,2,128,2,8]{4,2,6,5,3,1,0:T(8,128)S(1)} fusion(f32[128,2,2,8,128,1,1]{4,3,2,1,0,6,5:T(8,128)} %get-tuple-element.70, f32[1,128,8,9,2]{1,3,4,2,0:T(8,128)S(1)} %reverse_bitcast_fusion, f32[1,128,8,9,1]{1,3,4,2,0:T(8,128)S(1)} %get-tuple-element.61, f32[1,128,8,9,1]{1,3,4,2,0:T(8,128)S(1)} %get-tuple-element.60), kind=kOutput, calls=%fused_computation.30 | convolution fusion | flops 906043392 | bytes 4603904 | tf_op jit(solution)/shard_map/phxyz,hzcjt->hcpxyjt/dot_general | solution.py:80
  109.4 2.4 copy.139
  111.8 23.4 %all-to-all-done.1 = f32[16,128,2,8,9,2]{1,3,5,4,2,0:T(8,128)} async-done(((f32[16,128,2,8,9,2]{1,3,5,4,2,0:T(8,128)}), f32[16,128,2,8,9,2]{1,3,5,4,2,0:T(8,128)}, u32[]{:S(2)}, u32[]{:S(2)}) %all-to-all-start.1) | async-done | bytes 2359328 | tf_op jit(solution)/shard_map/all_to_all | solution.py:82
  135.3 5.7 %all-to-all-start.2 = ((f32[16,128,2,8,9,2]{1,3,5,4,2,0:T(8,128)}), f32[16,128,2,8,9,2]{1,3,5,4,2,0:T(8,128)}, u32[]{:S(2)}, u32[]{:S(2)}) async-start(f32[16,128,2,8,9,2]{1,3,5,4,2,0:T(8,128)} %copy.139), calls=%async_computation.2 | async-start | bytes 4718592 | tf_op jit(solution)/shard_map/all_to_all | solution.py:82
  141.1 6.1 %fusion.14 = f32[2,8,9,2,128,2,8]{4,2,6,5,3,1,0:T(8,128)S(1)} fusion(f32[128,2,2,8,128,1,1]{4,3,2,1,0,6,5:T(8,128)} %get-tuple-element.68, f32[1,128,8,9,2]{1,3,4,2,0:T(8,128)S(1)} %reverse_bitcast_fusion, f32[1,128,8,9,1]{1,3,4,2,0:T(8,128)S(1)} %get-tuple-element.61, f32[1,128,8,9,1]{1,3,4,2,0:T(8,128)S(1)} %get-tuple-element.60), kind=kOutput, calls=%fused_computation.28 | convolution fusion | flops 906043392 | bytes 4603904 | tf_op jit(solution)/shard_map/phxyz,hzcjt->hcpxyjt/dot_general | solution.py:80
  147.3 2.4 copy.148
  150.3 22.3 %all-to-all-done.2 = f32[16,128,2,8,9,2]{1,3,5,4,2,0:T(8,128)} async-done(((f32[16,128,2,8,9,2]{1,3,5,4,2,0:T(8,128)}), f32[16,128,2,8,9,2]{1,3,5,4,2,0:T(8,128)}, u32[]{:S(2)}, u32[]{:S(2)}) %all-to-all-start.2) | async-done | bytes 2359328 | tf_op jit(solution)/shard_map/all_to_all | solution.py:82
  172.6 6.1 %all-to-all-start.3 = ((f32[16,128,2,8,9,2]{1,3,5,4,2,0:T(8,128)}), f32[16,128,2,8,9,2]{1,3,5,4,2,0:T(8,128)}, u32[]{:S(2)}, u32[]{:S(2)}) async-start(f32[16,128,2,8,9,2]{1,3,5,4,2,0:T(8,128)} %copy.148), calls=%async_computation.3 | async-start | bytes 4718592 | tf_op jit(solution)/shard_map/all_to_all | solution.py:82
  181.9 2.9 fusion.111
  184.7 3.6 fusion.28
  190.2 5.3 %fusion.31 = f32[128,2,128,9,2]{0,2,3,1,4:T(8,128)S(1)} fusion(f32[16,128,2,8,9,2]{1,3,5,4,2,0:T(8,128)} %all-to-all-done.1, f32[16,8,1,128,1]{3,0,1,2,4:T(8,128)S(1)} %get-tuple-element.59, f32[16,8,1,128,1]{3,0,1,2,4:T(8,128)S(1)} %get-tuple-element.58, f32[16,8,1,128,1]{3,0,1,2,4:T(8,128)S(1)} %get-tuple-element.57), kind=kOutput, calls=%fused_computation.52 | convolution fusion | flops 1812135936 | bytes 4915200 | tf_op jit(solution)/shard_map/spxyjt,syteu->pxeju/dot_general | solution.py:83
  195.5 3.3 copy.132
  198.8 9.2 %gather_fusion.2 = f32[1024,128,2,2]{1,3,2,0:T(2,128)} fusion(f32[128,2,1152,2]{0,3,2,1:T(2,128)S(1)} %bitcast.189, s32[1024]{0:T(1024)S(1)} %broadcast_clamp_fusion), kind=kCustom, calls=%fused_computation.1.clone | custom fusion | bytes 4198400 | tf_op jit(solution)/shard_map/jit(_take)/gather | solution.py:85
  208.0 11.1 %gather_fusion.5 = f32[1024,128,2,2]{1,3,2,0:T(2,128)} fusion(f32[128,2,1152,2]{0,3,2,1:T(2,128)} %bitcast.190, s32[1024]{0:T(1024)S(1)} %broadcast_clamp_fusion), kind=kCustom, calls=%fused_computation.9.clone | custom fusion | bytes 4198400 | tf_op jit(solution)/shard_map/jit(_take)/gather | solution.py:85
  219.1 5.1 %fusion.34 = f32[128,2,128,9,2]{0,2,3,1,4:T(8,128)S(1)} fusion(f32[16,128,2,8,9,2]{1,3,5,4,2,0:T(8,128)} %all-to-all-done.2, f32[16,8,1,128,1]{3,0,1,2,4:T(8,128)S(1)} %copy-done.19, f32[16,8,1,128,1]{3,0,1,2,4:T(8,128)S(1)} %copy-done.17, f32[16,8,1,128,1]{3,0,1,2,4:T(8,128)S(1)} %copy-done.15), kind=kOutput, calls=%fused_computation.53 | convolution fusion | flops 1812135936 | bytes 4915200 | tf_op jit(solution)/shard_map/spxyjt,syteu->pxeju/dot_general | solution.py:83
  226.0 9.4 %gather_fusion.8 = f32[1024,128,2,2]{1,3,2,0:T(2,128)} fusion(f32[128,2,1152,2]{0,3,2,1:T(2,128)S(1)} %bitcast.192, s32[1024]{0:T(1024)S(1)} %broadcast_clamp_fusion), kind=kCustom, calls=%fused_computation.10.clone | custom fusion | bytes 4198400 | tf_op jit(solution)/shard_map/jit(_take)/gather | solution.py:85
  235.5 5.1 %fusion.37 = f32[128,2,128,9,2]{0,2,3,1,4:T(8,128)S(1)} fusion(f32[16,128,2,8,9,2]{1,3,5,4,2,0:T(8,128)} %all-to-all-done.3, f32[16,8,1,128,1]{3,0,1,2,4:T(8,128)S(1)} %copy-done.19, f32[16,8,1,128,1]{3,0,1,2,4:T(8,128)S(1)} %copy-done.17, f32[16,8,1,128,1]{3,0,1,2,4:T(8,128)S(1)} %copy-done.15), kind=kOutput, calls=%fused_computation.54 | convolution fusion | flops 1812135936 | bytes 4915200 | tf_op jit(solution)/shard_map/spxyjt,syteu->pxeju/dot_general | solution.py:83
  240.6 3.2 copy.150
  243.9 11.1 %gather_fusion.11 = f32[1024,128,2,2]{1,3,2,0:T(2,128)} fusion(f32[128,2,1152,2]{0,3,2,1:T(2,128)} %bitcast.191, s32[1024]{0:T(1024)S(1)} %broadcast_clamp_fusion), kind=kCustom, calls=%fused_computation.11.clone | custom fusion | bytes 4198400 | tf_op jit(solution)/shard_map/jit(_take)/gather | solution.py:85
  254.9 9.2 %select_bitcast_fusion = (f32[128,2,1024,2]{0,3,1,2:T(2,128)S(1)}, f32[128,2,1024,2]{0,3,1,2:T(2,128)}, f32[128,2,1024,2]{0,3,1,2:T(2,128)}, f32[128,2,1024,2]{0,3,1,2:T(2,128)}) fusion(f32[1024,128,2,2]{1,3,2,0:T(2,128)} %gather_fusion.11, pred[1024]{0:T(1024)(128)(4,1)S(1)} %copy-done.24, f32[1024,128,2,2]{1,3,2,0:T(2,128)} %gather_fusion.5, ...), kind=kLoop, calls=%fused_computation.39 | loop fusion | flops 2097152 | bytes 16778240 | tf_op jit(solution)/shard_map/jit(_take)/select_n | solution.py:85
  267.6 9.6 %add_reduce_fusion = (f32[128,1024]{0,1:T(8,128)}, f32[128,1024]{0,1:T(8,128)}) fusion(f32[128,2,1024]{0,1,2:T(2,128)S(1)} %copy.152, f32[128,2,1024]{0,1,2:T(2,128)S(1)} %bitcast.208, f32[2,1024]{0,1:T(8,128)} %get-tuple-element.79, f32[2,1024]{0,1:T(8,128)} %get-tuple-element.45), kind=kLoop, calls=%fused_computation.70 | loop fusion | flops 1835008 | bytes 3162112 | tf_op jit(solution)/shard_map/reduce_sum | solution.py:90
  277.2 2.2 copy.154
  281.4 2.6 fusion.107
  286.6 9.1 %add_reduce_fusion.1 = (f32[128,1024]{0,1:T(8,128)}, f32[128,1024]{0,1:T(8,128)}) fusion(f32[128,2,1024]{0,1,2:T(2,128)S(1)} %copy.143, f32[128,2,1024]{0,1,2:T(2,128)S(1)} %bitcast.209, f32[2,1024]{0,1:T(8,128)} %get-tuple-element.78, f32[2,1024]{0,1:T(8,128)} %get-tuple-element.46), kind=kLoop, calls=%fused_computation.72 | loop fusion | flops 1835008 | bytes 3162112 | tf_op jit(solution)/shard_map/reduce_sum | solution.py:90
  299.9 2.6 fusion.108
  305.1 9.1 %add_reduce_fusion.2 = (f32[128,1024]{0,1:T(8,128)}, f32[128,1024]{0,1:T(8,128)}) fusion(f32[128,2,1024]{0,1,2:T(2,128)S(1)} %copy.134, f32[128,2,1024]{0,1,2:T(2,128)S(1)} %bitcast.210, f32[2,1024]{0,1:T(8,128)} %get-tuple-element.77, f32[2,1024]{0,1:T(8,128)} %get-tuple-element.47), kind=kLoop, calls=%fused_computation.74 | loop fusion | flops 1835008 | bytes 3162112 | tf_op jit(solution)/shard_map/reduce_sum | solution.py:90
  314.2 2.2 copy.136
  318.5 2.6 fusion.109
  323.6 9.3 %add_reduce_fusion.3 = (f32[128,1024]{0,1:T(8,128)}, f32[128,1024]{0,1:T(8,128)}) fusion(f32[128,2,1024]{0,1,2:T(2,128)S(1)} %copy.125, f32[128,2,1024]{0,1,2:T(2,128)S(1)} %bitcast.207, f32[2,1024]{0,1:T(8,128)} %get-tuple-element.76, f32[2,1024]{0,1:T(8,128)} %get-tuple-element.48), kind=kLoop, calls=%fused_computation.76 | loop fusion | flops 1835008 | bytes 3162112 | tf_op jit(solution)/shard_map/reduce_sum | solution.py:90
  335.6 2.5 fusion.44
  338.1 5.3 %all-to-all-start.4 = ((f32[8,2,128,128]{3,2,1,0:T(8,128)}), f32[8,2,128,128]{3,2,1,0:T(8,128)S(1)}, u32[]{:S(2)}, u32[]{:S(2)}) async-start(f32[8,2,128,128]{3,2,1,0:T(8,128)} %fusion.44), calls=%async_computation.4 | async-start | bytes 2097152 | tf_op jit(solution)/shard_map/all_to_all | solution.py:97
  343.5 16.0 %all-to-all-done.4 = f32[8,2,128,128]{3,2,1,0:T(8,128)S(1)} async-done(((f32[8,2,128,128]{3,2,1,0:T(8,128)}), f32[8,2,128,128]{3,2,1,0:T(8,128)S(1)}, u32[]{:S(2)}, u32[]{:S(2)}) %all-to-all-start.4) | async-done | bytes 1048608 | tf_op jit(solution)/shard_map/all_to_all | solution.py:97
  359.6 2.7 collective-permute-start
  362.3 5.0 %collective-permute-done = f32[2,128,64]{1,2,0:T(8,128)S(1)} collective-permute-done((f32[2,128,64]{1,2,0:T(8,128)S(1)}, f32[2,128,64]{1,2,0:T(8,128)S(1)}, u32[]{:S(2)}, u32[]{:S(2)}) %collective-permute-start) | collective-permute-done | bytes 65568 | tf_op jit(solution)/shard_map/ppermute | solution.py:101
  368.4 6.6 %all-to-all-start.5 = ((f32[16,2,128,64]{2,3,1,0:T(8,128)}), f32[16,2,128,64]{2,3,1,0:T(8,128)S(1)}, u32[]{:S(2)}, u32[]{:S(2)}) async-start(f32[16,2,128,64]{2,3,1,0:T(8,128)} %broadcast_in_dim.47), calls=%async_computation.5 | async-start | bytes 2097152 | tf_op jit(solution)/shard_map/all_to_all | solution.py:104
  375.1 13.5 %all-to-all-done.5 = f32[16,2,128,64]{2,3,1,0:T(8,128)S(1)} async-done(((f32[16,2,128,64]{2,3,1,0:T(8,128)}), f32[16,2,128,64]{2,3,1,0:T(8,128)S(1)}, u32[]{:S(2)}, u32[]{:S(2)}) %all-to-all-start.5) | async-done | bytes 1048608 | tf_op jit(solution)/shard_map/all_to_all | solution.py:104
  388.7 4.7 %collective-permute-start.1 = (f32[2,128,512]{1,2,0:T(8,128)S(1)}, f32[2,128,512]{1,2,0:T(8,128)S(1)}, u32[]{:S(2)}, u32[]{:S(2)}) collective-permute-start(f32[2,128,512]{1,2,0:T(8,128)S(1)} %constant_dynamic-slice_fusion), channel_id=1, source_target_pairs={{0,0},{1,16},{2,32},{3,48},{4,64},{5,80},{6,96},{7,112},{8,1},{9,1... | collective-permute-start | bytes 1572872 | tf_op jit(solution)/shard_map/ppermute | solution.py:114
  393.7 45.8 %collective-permute-done.1 = f32[2,128,512]{1,2,0:T(8,128)S(1)} collective-permute-done((f32[2,128,512]{1,2,0:T(8,128)S(1)}, f32[2,128,512]{1,2,0:T(8,128)S(1)}, u32[]{:S(2)}, u32[]{:S(2)}) %collective-permute-start.1) | collective-permute-done | bytes 524320 | tf_op jit(solution)/shard_map/ppermute | solution.py:114
  447.2 2.5 pad_maximum_fusion
  (122 shorter events, 63.7 us)
Async XLA Ops:
  2.1 3.8 copy-start.6
  26.8 2.0 copy-start.2
  44.4 53.2 %all-to-all-start = ((f32[16,128,2,8,9,2]{1,3,5,4,2,0:T(8,128)}), f32[16,128,2,8,9,2]{1,3,5,4,2,0:T(8,128)S(1)}, u32[]{:S(2)}, u32[]{:S(2)}) async-start(f32[16,128,2,8,9,2]{1,3,5,4,2,0:T(8,128)} %copy.121), calls=%async_computation | async-start | bytes 4718592 | tf_op jit(solution)/shard_map/all_to_all | solution.py:82
  97.6 37.6 %all-to-all-start.1 = ((f32[16,128,2,8,9,2]{1,3,5,4,2,0:T(8,128)}), f32[16,128,2,8,9,2]{1,3,5,4,2,0:T(8,128)}, u32[]{:S(2)}, u32[]{:S(2)}) async-start(f32[16,128,2,8,9,2]{1,3,5,4,2,0:T(8,128)} %copy.130), calls=%async_computation.1 | async-start | bytes 4718592 | tf_op jit(solution)/shard_map/all_to_all | solution.py:82
  111.8 29.1 %copy-start.21 = (s32[8192]{0:T(1024)S(1)}, s32[8192]{0:T(1024)}, u32[]{:S(2)}) copy-start(s32[8192]{0:T(1024)} %param.18) | copy-start | bytes 98308
  135.3 37.3 %all-to-all-start.2 = ((f32[16,128,2,8,9,2]{1,3,5,4,2,0:T(8,128)}), f32[16,128,2,8,9,2]{1,3,5,4,2,0:T(8,128)}, u32[]{:S(2)}, u32[]{:S(2)}) async-start(f32[16,128,2,8,9,2]{1,3,5,4,2,0:T(8,128)} %copy.139), calls=%async_computation.2 | async-start | bytes 4718592 | tf_op jit(solution)/shard_map/all_to_all | solution.py:82
  172.6 62.9 %all-to-all-start.3 = ((f32[16,128,2,8,9,2]{1,3,5,4,2,0:T(8,128)}), f32[16,128,2,8,9,2]{1,3,5,4,2,0:T(8,128)}, u32[]{:S(2)}, u32[]{:S(2)}) async-start(f32[16,128,2,8,9,2]{1,3,5,4,2,0:T(8,128)} %copy.148), calls=%async_computation.3 | async-start | bytes 4718592 | tf_op jit(solution)/shard_map/all_to_all | solution.py:82
  179.7 10.5 %copy-start.14 = (f32[16,8,1,128,1]{3,0,1,2,4:T(8,128)}, f32[16,8,1,128,1]{3,0,1,2,4:T(8,128)S(1)}, u32[]{:S(2)}) copy-start(f32[16,8,1,128,1]{3,0,1,2,4:T(8,128)S(1)} %get-tuple-element.57) | copy-start | bytes 196612
  179.7 10.5 %copy-start.16 = (f32[16,8,1,128,1]{3,0,1,2,4:T(8,128)}, f32[16,8,1,128,1]{3,0,1,2,4:T(8,128)S(1)}, u32[]{:S(2)}) copy-start(f32[16,8,1,128,1]{3,0,1,2,4:T(8,128)S(1)} %get-tuple-element.58) | copy-start | bytes 196612
  179.7 10.5 %copy-start.18 = (f32[16,8,1,128,1]{3,0,1,2,4:T(8,128)}, f32[16,8,1,128,1]{3,0,1,2,4:T(8,128)S(1)}, u32[]{:S(2)}) copy-start(f32[16,8,1,128,1]{3,0,1,2,4:T(8,128)S(1)} %get-tuple-element.59) | copy-start | bytes 196612
  208.0 11.1 %copy-start.15 = (f32[16,8,1,128,1]{3,0,1,2,4:T(8,128)S(1)}, f32[16,8,1,128,1]{3,0,1,2,4:T(8,128)}, u32[]{:S(2)}) copy-start(f32[16,8,1,128,1]{3,0,1,2,4:T(8,128)} %copy-done.14) | copy-start | bytes 196612
  208.0 11.1 %copy-start.17 = (f32[16,8,1,128,1]{3,0,1,2,4:T(8,128)S(1)}, f32[16,8,1,128,1]{3,0,1,2,4:T(8,128)}, u32[]{:S(2)}) copy-start(f32[16,8,1,128,1]{3,0,1,2,4:T(8,128)} %copy-done.16) | copy-start | bytes 196612
  208.0 11.1 %copy-start.19 = (f32[16,8,1,128,1]{3,0,1,2,4:T(8,128)S(1)}, f32[16,8,1,128,1]{3,0,1,2,4:T(8,128)}, u32[]{:S(2)}) copy-start(f32[16,8,1,128,1]{3,0,1,2,4:T(8,128)} %copy-done.18) | copy-start | bytes 196612
  243.8 11.1 %copy-start = (f32[1024,128,2,2]{1,3,2,0:T(2,128)S(1)}, f32[1024,128,2,2]{1,3,2,0:T(2,128)}, u32[]{:S(2)}) copy-start(f32[1024,128,2,2]{1,3,2,0:T(2,128)} %gather_fusion.2) | copy-start | bytes 6291460
  243.9 11.1 %copy-start.24 = (pred[1024]{0:T(1024)(128)(4,1)S(1)}, pred[1024]{0:T(1024)(128)(4,1)}, u32[]{:S(2)}) copy-start(pred[1024]{0:T(1024)(128)(4,1)} %get-tuple-element.15) | copy-start | bytes 3076
  277.2 4.2 copy-start.4
  285.3 1.2 copy-start.8
  295.7 4.2 copy-start.3
  303.8 1.2 copy-start.9
  314.2 4.2 copy-start.1
  322.4 1.2 copy-start.7
  323.6 12.0 %copy-start.20 = (f32[2,8,128]{2,0,1:T(2,128)S(1)}, f32[2,8,128]{2,0,1:T(2,128)}, u32[]{:S(2)}) copy-start(f32[2,8,128]{2,0,1:T(2,128)} %pad_bitcast_fusion) | copy-start | bytes 24580
  332.9 2.7 copy-start.10
  332.9 2.7 copy-start.11
  332.9 2.7 copy-start.12
  332.9 2.7 copy-start.13
  338.1 21.3 %all-to-all-start.4 = ((f32[8,2,128,128]{3,2,1,0:T(8,128)}), f32[8,2,128,128]{3,2,1,0:T(8,128)S(1)}, u32[]{:S(2)}, u32[]{:S(2)}) async-start(f32[8,2,128,128]{3,2,1,0:T(8,128)} %fusion.44), calls=%async_computation.4 | async-start | bytes 2097152 | tf_op jit(solution)/shard_map/all_to_all | solution.py:97
  359.6 7.7 %collective-permute-start = (f32[2,128,64]{1,2,0:T(8,128)S(1)}, f32[2,128,64]{1,2,0:T(8,128)S(1)}, u32[]{:S(2)}, u32[]{:S(2)}) collective-permute-start(f32[2,128,64]{1,2,0:T(8,128)S(1)} %dynamic-slice_bitcast_fusion), channel_id=1, source_target_pairs={{0,15},{1,14},{2,13},{3,12},{4,11},{5,10},{6,9},{7,8},{8,7},{9,6},... | collective-permute-start | bytes 196616 | tf_op jit(solution)/shard_map/ppermute | solution.py:101
  368.4 20.2 %all-to-all-start.5 = ((f32[16,2,128,64]{2,3,1,0:T(8,128)}), f32[16,2,128,64]{2,3,1,0:T(8,128)S(1)}, u32[]{:S(2)}, u32[]{:S(2)}) async-start(f32[16,2,128,64]{2,3,1,0:T(8,128)} %broadcast_in_dim.47), calls=%async_computation.5 | async-start | bytes 2097152 | tf_op jit(solution)/shard_map/all_to_all | solution.py:104
  375.0 18.4 %copy-start.22 = (s32[128]{0:T(128)S(1)}, s32[128]{0:T(128)}, u32[]{:S(2)}) copy-start(s32[128]{0:T(128)} %param.17) | copy-start | bytes 1540
  375.0 18.4 %copy-start.23 = (s32[128]{0:T(128)S(1)}, s32[128]{0:T(128)}, u32[]{:S(2)}) copy-start(s32[128]{0:T(128)} %param.16) | copy-start | bytes 1540
  375.0 18.4 %copy-start.25 = (f32[64]{0:T(128)S(1)}, f32[64]{0:T(128)}, u32[]{:S(2)}) copy-start(f32[64]{0:T(128)} %param.14) | copy-start | bytes 772
  375.1 18.4 %copy-start.26 = (f32[64]{0:T(128)S(1)}, f32[64]{0:T(128)}, u32[]{:S(2)}) copy-start(f32[64]{0:T(128)} %param.15) | copy-start | bytes 772
  388.7 50.8 %collective-permute-start.1 = (f32[2,128,512]{1,2,0:T(8,128)S(1)}, f32[2,128,512]{1,2,0:T(8,128)S(1)}, u32[]{:S(2)}, u32[]{:S(2)}) collective-permute-start(f32[2,128,512]{1,2,0:T(8,128)S(1)} %constant_dynamic-slice_fusion), channel_id=1, source_target_pairs={{0,0},{1,16},{2,32},{3,48},{4,64},{5,80},{6,96},{7,112},{8,1},{9,1... | collective-permute-start | bytes 1572872 | tf_op jit(solution)/shard_map/ppermute | solution.py:114
  439.5 3.6 copy-start.5
